TPU v7x, 32 devices: a whole 2x2x4 slice. The times are simulated.
32 devices in a mesh: group: 2 (over y), seq: 4 (over z), batch: 2 (over x), chan: 2 (over core).
Axes of the slice: x: 2, y: 2, z: 4, core: 2. Of those that a mesh axis runs over, the one named last changes fastest.
Arguments:
- history: bfloat16 [8, 1024, 4096], P(('group', 'batch'), 'seq', 'chan'), parts along dimension 0, may hold values from -6 to 6
- filter_taps: bfloat16 [1024, 4096], P('seq', 'chan'), may hold values from -0.1875 to 0.1875
- lengths: int32 [8], P(('group', 'batch')), parts along dimension 0, may hold values from 256 to 1024, as said below
- inner_gate: bfloat16 [8, 256, 4096], P(('group', 'batch'), 'seq', 'chan'), parts along dimension 0, may hold values from -6 to 6
- values_in: bfloat16 [8, 256, 4096], P(('group', 'batch'), 'seq', 'chan'), parts along dimension 0, may hold values from -6 to 6
- outer_gate: bfloat16 [8, 256, 4096], P(('group', 'batch'), 'seq', 'chan'), parts along dimension 0, may hold values from -6 to 6
- skip_gain: float32 [4096], P('chan'), may hold values from -4 to 4
Outputs:
- mixed: bfloat16 [8, 256, 4096], P(('group', 'batch'), 'seq', 'chan'), parts along dimension 0
- next_history: bfloat16 [8, 1024, 4096], P(('group', 'batch'), 'seq', 'chan'), parts along dimension 0
There are 2 independent parts, one for each index of `group`. A program takes and returns all parts, laid end to end along the dimension named above; an argument that names none is the same for every part. Nothing has to cross between parts.
Inputs may be any that keep to these rules, and one draw needn't show every extreme that they name: `lengths`: each request's prefilled length is a multiple of 256; some request of every part has exactly 1024, and some other is shorter.
All inputs are finite; a program needn't handle non-finite values.
Results may differ from a plain program's by a relative error of at most 0.0044.
Values may be sent and summed in bfloat16 or wider, within the bound.
No kernel may reach another device: no remote copies, remote signals or barrier semaphores. Data moves between devices by JAX's collectives and lax.ppermute only.
A program may use at most 128 MiB of HBM per device.

v0:
```python
import jax
import jax.numpy as jnp
from jax import lax
from jax.sharding import PartitionSpec as P

CHUNK_PARTS = (1, 3, 3, 1)


def from_behind(block, axis, distance):
    devices = range(lax.axis_size(axis))
    route = [(i - distance, i) for i in devices if i - distance in devices]
    return lax.ppermute(block, axis, route)


def correlate(signal, kernel):
    width = signal.shape[2]
    return lax.conv_general_dilated(
        signal,
        kernel[:, None, :],
        (1,),
        "VALID",
        dimension_numbers=("NWC", "WIO", "NWC"),
        feature_group_count=width,
        preferred_element_type=jnp.float32,
    )


def per_device(history, filter_taps, lengths, inner_gate, values_in, outer_gate, skip_gain):
    position = lax.axis_index("seq")
    n_seq = lax.axis_size("seq")
    requests, tile_len, width = history.shape
    own_tokens = inner_gate.shape[1]
    span_len = own_tokens * n_seq
    assert span_len == tile_len
    unit = width // sum(CHUNK_PARTS)
    bounds = [0]
    for parts in CHUNK_PARTS:
        bounds.append(bounds[-1] + parts * unit)
    chunk = bounds[1]
    product_own = (inner_gate.astype(jnp.float32) * values_in.astype(jnp.float32)).astype(
        jnp.bfloat16
    )
    token_ids = jnp.arange(own_tokens, dtype=jnp.int32)
    exchange = (token_ids[:, None] + token_ids[None, :] == own_tokens - 1).astype(jnp.bfloat16)
    product_own = lax.optimization_barrier(product_own)
    product_rev = jnp.einsum(
        "ik,rkc->ric", exchange, product_own, preferred_element_type=jnp.float32
    ).astype(jnp.bfloat16)
    first_each = [product_rev[:, :, :chunk]] + [
        lax.ppermute(product_rev[:, :, :chunk], "seq", [(d, 0)]) for d in range(1, n_seq)
    ]
    rest_each = [product_rev[:, :, chunk:]] + [
        lax.ppermute(product_rev[:, :, chunk:], "seq", [(d, 0)]) for d in range(1, n_seq)
    ]
    row_ids = position * tile_len + jnp.arange(tile_len, dtype=jnp.int32)
    live_rows = jnp.where(
        (row_ids[None, :] < lengths[:, None])[:, :, None], history, jnp.zeros_like(history)
    )
    prev_keep = ((row_ids - tile_len)[None, :] < lengths[:, None])[:, :, None]

    head_parts = []
    own_parts = []
    for c in range(len(CHUNK_PARTS)):
        cols = slice(bounds[c], bounds[c + 1])
        sent = from_behind(history[:, :, cols], "seq", 1)
        if own_parts:
            (sent, rest_each), _ = lax.optimization_barrier(((sent, rest_each), last_partial))
            rest_cols = slice(bounds[c] - chunk, bounds[c + 1] - chunk)
            head_first = jnp.concatenate(
                [part[:, :, rest_cols] for part in rest_each[::-1]], axis=1
            )
        else:
            head_first = jnp.concatenate(first_each[::-1], axis=1)
        head_c = jnp.where(position == 0, head_first, sent)
        head_parts.append(head_c)
        prev_live = jnp.where(prev_keep, head_c, jnp.zeros_like(head_c))
        segment = jnp.concatenate([prev_live, live_rows[:, : tile_len - 1, cols]], axis=1)
        partial_rev = correlate(segment, filter_taps[:, cols])
        last_partial = partial_rev
        blocks = partial_rev.reshape(requests, n_seq, own_tokens, -1)[:, ::-1]
        if own_parts:
            blocks, _ = lax.optimization_barrier((blocks, own_parts[-1]))
        reduced = lax.psum_scatter(blocks, "seq", scatter_dimension=1, tiled=True)
        own_parts.append(reduced[:, 0])
    summed = jnp.einsum(
        "ik,rkc->ric",
        exchange.astype(jnp.float32),
        jnp.concatenate(own_parts, axis=2),
        precision=lax.Precision.HIGHEST,
        preferred_element_type=jnp.float32,
    )
    product_float = product_own.astype(jnp.float32)
    total = summed + skip_gain[None, None, :] * product_float
    mixed = (outer_gate.astype(jnp.float32) * total).astype(jnp.bfloat16)
    next_history = jnp.concatenate(head_parts, axis=2)
    return (mixed, next_history)


def solution(mesh):
    in_specs = (
        P(("group", "batch"), "seq", "chan"),
        P("seq", "chan"),
        P(("group", "batch")),
        P(("group", "batch"), "seq", "chan"),
        P(("group", "batch"), "seq", "chan"),
        P(("group", "batch"), "seq", "chan"),
        P("chan"),
    )
    out_specs = (P(("group", "batch"), "seq", "chan"), P(("group", "batch"), "seq", "chan"))
    return jax.shard_map(
        per_device, mesh=mesh, in_specs=in_specs, out_specs=out_specs, check_vma=False
    )
```

profile of v0, /device:TPU:0, one launch (start us, length us, event | category | flops | bytes accessed | tf_op | source)
XLA Modules:
  0.0 229.3 jit_solution(14480016477273774620)
XLA Ops:
  7.2 1.5 multiply_convert_fusion
  10.9 1.3 collective-permute-start.1
  12.2 1.3 collective-permute-start
  16.5 6.3 %collective-permute-start.3 = (bf16[2,256,256]{2,1,0:T(8,128)(2,1)}, bf16[2,256,256]{2,1,0:T(8,128)(2,1)}, u32[]{:S(2)}, u32[]{:S(2)}) collective-permute-start(bf16[2,256,256]{2,1,0:T(8,128)(2,1)} %get-tuple-element.48), channel_id=1, source_target_pairs={{0,4},{4,8},{8,12},{1,5},{5,9},{9,13},{2,6},{6,10},{10,14},{3,7},{... | collective-permute-start | bytes 786440 | tf_op jit(solution)/shard_map/ppermute | solution.py:12
  26.5 1.6 slice_bitcast_fusion.2
  29.4 1.3 collective-permute-start.5
  30.7 6.2 %collective-permute-start.4 = (bf16[2,256,768]{2,1,0:T(8,128)(2,1)}, bf16[2,256,768]{2,1,0:T(8,128)(2,1)}, u32[]{:S(2)}, u32[]{:S(2)}) collective-permute-start(bf16[2,256,768]{2,1,0:T(8,128)(2,1)} %get-tuple-element.52), channel_id=1, source_target_pairs={{0,4},{4,8},{8,12},{1,5},{5,9},{9,13},{2,6},{6,10},{10,14},{3,7},{... | collective-permute-start | bytes 2359304 | tf_op jit(solution)/shard_map/ppermute | solution.py:12
  36.9 2.8 %collective-permute-start.8 = (bf16[2,256,768]{2,1,0:T(8,128)(2,1)}, bf16[2,256,768]{2,1,0:T(8,128)(2,1)}, u32[]{:S(2)}, u32[]{:S(2)}) collective-permute-start(bf16[2,256,768]{2,1,0:T(8,128)(2,1)} %get-tuple-element.53), channel_id=1, source_target_pairs={{0,4},{4,8},{8,12},{1,5},{5,9},{9,13},{2,6},{6,10},{10,14},{3,7},{... | collective-permute-start | bytes 2359304 | tf_op jit(solution)/shard_map/ppermute | solution.py:12
  39.7 1.7 broadcast_select_fusion.4
  41.5 14.5 %fusion.19 = f32[2,256,256]{2,0,1:T(2,128)S(1)} fusion(bf16[2,511,256]{2,1,0:T(8,128)(2,1)S(1)} %pad_maximum_fusion.3, bf16[256,1,256]{2,0,1:T(8,128)(2,1)S(1)} %get-tuple-element.55), kind=kOutput, calls=%fused_computation.32 | convolution fusion | flops 67108864 | bytes 1178624 | tf_op jit(solution)/shard_map/conv_general_dilated | solution.py:17
  61.5 43.6 %fusion.6 = f32[2,256,768]{2,0,1:T(2,128)S(1)} fusion(bf16[2,511,768]{2,1,0:T(8,128)(2,1)S(1)} %pad_maximum_fusion.1, bf16[256,1,768]{2,0,1:T(8,128)(2,1)S(1)} %get-tuple-element.57), kind=kOutput, calls=%fused_computation.12 | convolution fusion | flops 201326592 | bytes 3535872 | tf_op jit(solution)/shard_map/conv_general_dilated | solution.py:17
  106.0 1.6 slice.99
  107.6 1.6 slice.100
  109.4 1.3 rev.13
  110.8 1.3 broadcast_select_fusion.1
  113.2 43.6 %fusion.4 = f32[2,256,768]{2,0,1:T(2,128)S(1)} fusion(bf16[2,511,768]{2,1,0:T(8,128)(2,1)S(1)} %pad_maximum_fusion.2, bf16[256,1,768]{2,0,1:T(8,128)(2,1)S(1)} %copy-done.8), kind=kOutput, calls=%fused_computation.10 | convolution fusion | flops 201326592 | bytes 3535872 | tf_op jit(solution)/shard_map/conv_general_dilated | solution.py:17
  156.9 1.3 rev.14
  159.1 3.0 %collective-permute-start.9 = (bf16[2,256,256]{2,1,0:T(8,128)(2,1)S(1)}, bf16[2,256,256]{2,1,0:T(8,128)(2,1)S(1)}, u32[]{:S(2)}, u32[]{:S(2)}) collective-permute-start(bf16[2,256,256]{2,1,0:T(8,128)(2,1)S(1)} %copy-done.9), channel_id=1, source_target_pairs={{0,4},{4,8},{8,12},{1,5},{5,9},{9,13},{2,6},{6,10},{10,14},{3,7},{... | collective-permute-start | bytes 786440 | tf_op jit(solution)/shard_map/ppermute | solution.py:12
  162.1 8.8 %collective-permute-done.9 = bf16[2,256,256]{2,1,0:T(8,128)(2,1)S(1)} collective-permute-done((bf16[2,256,256]{2,1,0:T(8,128)(2,1)S(1)}, bf16[2,256,256]{2,1,0:T(8,128)(2,1)S(1)}, u32[]{:S(2)}, u32[]{:S(2)}) %collective-permute-start.9) | collective-permute-done | bytes 262176 | tf_op jit(solution)/shard_map/ppermute | solution.py:12
  173.6 14.5 %fusion.17 = f32[2,256,256]{2,0,1:T(2,128)S(1)} fusion(bf16[2,511,256]{2,1,0:T(8,128)(2,1)S(1)} %pad_maximum_fusion.4, bf16[256,1,256]{2,0,1:T(8,128)(2,1)S(1)} %copy-done.10), kind=kOutput, calls=%fused_computation.30 | convolution fusion | flops 67108864 | bytes 1178624 | tf_op jit(solution)/shard_map/conv_general_dilated | solution.py:17
  189.0 4.4 %reduce-scatter.9.cloned.1.call-done = f32[2,1,64,768]{3,2,0,1:T(8,128)} async-done(((f32[2,4,64,768]{3,2,0,1:T(8,128)}), f32[2,1,64,768]{3,2,0,1:T(8,128)}) %reduce-scatter.9.cloned.1.call-update) | async-done | bytes 393232 | tf_op jit(solution)/shard_map/reduce_scatter | solution.py:83
  193.5 1.6 pad_maximum_fusion
  195.2 24.8 %reduce-scatter.11.cloned.1.call-done = f32[2,1,64,256]{3,2,0,1:T(8,128)} async-done(((f32[2,4,64,256]{3,2,0,1:T(8,128)}), f32[2,1,64,256]{3,2,0,1:T(8,128)}) %reduce-scatter.11.cloned.1.call-update) | async-done | bytes 131088 | tf_op jit(solution)/shard_map/reduce_scatter | solution.py:83
  220.0 2.7 %fusion.2 = bf16[2,64,2048]{2,1,0:T(8,128)(2,1)} fusion(f32[2,64,256]{2,1,0:T(8,128)} %bitcast.38, f32[2,64,768]{2,1,0:T(8,128)} %bitcast.36, f32[2,64,768]{2,1,0:T(8,128)S(1)} %bitcast.35, f32[2,64,256]{2,1,0:T(8,128)} %bitcast.37, bf16[2,64,2048]{2,1,0:T(8,128)(2,1)S(1)} %copy-done.3, bf16[2,64,2048]{2,1,0:T(8,128)(2,1)S(1)} %copy-done.12, ...), kind=kOutput, calls=%fused_computation.3 | convolution fusion | flops 203694080 | bytes 2629632 | tf_op jit(solution)/shard_map/ik,rkc->ric/dot_general | solution.py:85
  (87 shorter events, 22.4 us)
Async XLA Ops:
  7.2 8.5 %copy-start = (bf16[2,256,2048]{2,1,0:T(8,128)(2,1)S(1)}, bf16[2,256,2048]{2,1,0:T(8,128)(2,1)}, u32[]{:S(2)}) copy-start(bf16[2,256,2048]{2,1,0:T(8,128)(2,1)} %param.7) | copy-start | bytes 6291460
  7.2 105.0 %reduce-scatter.5.cloned.1.call-start = ((), (), s32[]{:S(2)}) async-start(), calls=%async_computation.4 | async-start | bytes 655360 | tf_op jit(solution)/shard_map/reduce_scatter | solution.py:83
  8.7 7.8 %copy-start.2 = (bf16[2,64,2048]{2,1,0:T(8,128)(2,1)}, bf16[2,64,2048]{2,1,0:T(8,128)(2,1)S(1)}, u32[]{:S(2)}) copy-start(bf16[2,64,2048]{2,1,0:T(8,128)(2,1)S(1)} %multiply_convert_fusion) | copy-start | bytes 1572868
  9.6 18.5 %collective-permute-start.2 = (bf16[2,64,256]{2,1,0:T(8,128)(2,1)}, bf16[2,64,256]{2,1,0:T(8,128)(2,1)}, u32[]{:S(2)}, u32[]{:S(2)}) collective-permute-start(bf16[2,64,256]{2,1,0:T(8,128)(2,1)} %slice.110), channel_id=1, source_target_pairs={{4,0},{5,1},{6,2},{7,3},{20,16},{21,17},{22,18},{23,19}} | collective-permute-start | bytes 196616 | tf_op jit(solution)/shard_map/ppermute | solution.py:50
  10.9 18.5 %collective-permute-start.1 = (bf16[2,64,256]{2,1,0:T(8,128)(2,1)}, bf16[2,64,256]{2,1,0:T(8,128)(2,1)}, u32[]{:S(2)}, u32[]{:S(2)}) collective-permute-start(bf16[2,64,256]{2,1,0:T(8,128)(2,1)} %slice.110), channel_id=1, source_target_pairs={{8,0},{9,1},{10,2},{11,3},{24,16},{25,17},{26,18},{27,19}} | collective-permute-start | bytes 196616 | tf_op jit(solution)/shard_map/ppermute | solution.py:50
  12.2 18.5 %collective-permute-start = (bf16[2,64,256]{2,1,0:T(8,128)(2,1)}, bf16[2,64,256]{2,1,0:T(8,128)(2,1)}, u32[]{:S(2)}, u32[]{:S(2)}) collective-permute-start(bf16[2,64,256]{2,1,0:T(8,128)(2,1)} %slice.110), channel_id=1, source_target_pairs={{12,0},{13,1},{14,2},{15,3},{28,16},{29,17},{30,18},{31,19}} | collective-permute-start | bytes 196616 | tf_op jit(solution)/shard_map/ppermute | solution.py:50
  14.3 42.8 %collective-permute-start.7 = (bf16[2,64,1792]{2,1,0:T(8,128)(2,1)}, bf16[2,64,1792]{2,1,0:T(8,128)(2,1)}, u32[]{:S(2)}, u32[]{:S(2)}) collective-permute-start(bf16[2,64,1792]{2,1,0:T(8,128)(2,1)} %slice.112), channel_id=1, source_target_pairs={{12,0},{13,1},{14,2},{15,3},{28,16},{29,17},{30,18},{31,19}} | collective-permute-start | bytes 1376264 | tf_op jit(solution)/shard_map/ppermute | solution.py:53
  16.5 20.4 %collective-permute-start.3 = (bf16[2,256,256]{2,1,0:T(8,128)(2,1)}, bf16[2,256,256]{2,1,0:T(8,128)(2,1)}, u32[]{:S(2)}, u32[]{:S(2)}) collective-permute-start(bf16[2,256,256]{2,1,0:T(8,128)(2,1)} %get-tuple-element.48), channel_id=1, source_target_pairs={{0,4},{4,8},{8,12},{1,5},{5,9},{9,13},{2,6},{6,10},{10,14},{3,7},{... | collective-permute-start | bytes 786440 | tf_op jit(solution)/shard_map/ppermute | solution.py:12
  28.1 29.0 %collective-permute-start.6 = (bf16[2,64,1792]{2,1,0:T(8,128)(2,1)}, bf16[2,64,1792]{2,1,0:T(8,128)(2,1)S(1)}, u32[]{:S(2)}, u32[]{:S(2)}) collective-permute-start(bf16[2,64,1792]{2,1,0:T(8,128)(2,1)} %slice.112), channel_id=1, source_target_pairs={{8,0},{9,1},{10,2},{11,3},{24,16},{25,17},{26,18},{27,19}} | collective-permute-start | bytes 1376264 | tf_op jit(solution)/shard_map/ppermute | solution.py:53
  29.4 27.8 %collective-permute-start.5 = (bf16[2,64,1792]{2,1,0:T(8,128)(2,1)}, bf16[2,64,1792]{2,1,0:T(8,128)(2,1)}, u32[]{:S(2)}, u32[]{:S(2)}) collective-permute-start(bf16[2,64,1792]{2,1,0:T(8,128)(2,1)} %slice.112), channel_id=1, source_target_pairs={{4,0},{5,1},{6,2},{7,3},{20,16},{21,17},{22,18},{23,19}} | collective-permute-start | bytes 1376264 | tf_op jit(solution)/shard_map/ppermute | solution.py:53
  30.7 26.5 %collective-permute-start.4 = (bf16[2,256,768]{2,1,0:T(8,128)(2,1)}, bf16[2,256,768]{2,1,0:T(8,128)(2,1)}, u32[]{:S(2)}, u32[]{:S(2)}) collective-permute-start(bf16[2,256,768]{2,1,0:T(8,128)(2,1)} %get-tuple-element.52), channel_id=1, source_target_pairs={{0,4},{4,8},{8,12},{1,5},{5,9},{9,13},{2,6},{6,10},{10,14},{3,7},{... | collective-permute-start | bytes 2359304 | tf_op jit(solution)/shard_map/ppermute | solution.py:12
  36.9 68.1 %collective-permute-start.8 = (bf16[2,256,768]{2,1,0:T(8,128)(2,1)}, bf16[2,256,768]{2,1,0:T(8,128)(2,1)}, u32[]{:S(2)}, u32[]{:S(2)}) collective-permute-start(bf16[2,256,768]{2,1,0:T(8,128)(2,1)} %get-tuple-element.53), channel_id=1, source_target_pairs={{0,4},{4,8},{8,12},{1,5},{5,9},{9,13},{2,6},{6,10},{10,14},{3,7},{... | collective-permute-start | bytes 2359304 | tf_op jit(solution)/shard_map/ppermute | solution.py:12
  56.9 101.3 %reduce-scatter.7.cloned.1.call-start = ((), (), s32[]{:S(2)}) async-start(), calls=%async_computation.5 | async-start | bytes 1966080 | tf_op jit(solution)/shard_map/reduce_scatter | solution.py:83
  57.2 48.9 %copy-start.7 = (bf16[2,64,1792]{2,1,0:T(8,128)(2,1)}, bf16[2,64,1792]{2,1,0:T(8,128)(2,1)S(1)}, u32[]{:S(2)}) copy-start(bf16[2,64,1792]{2,1,0:T(8,128)(2,1)S(1)} %collective-permute-done.6) | copy-start | bytes 1376260
  112.2 81.2 %reduce-scatter.9.cloned.1.call-start = ((), (), s32[]{:S(2)}) async-start(), calls=%async_computation.6 | async-start | bytes 1966080 | tf_op jit(solution)/shard_map/reduce_scatter | solution.py:83
  158.2 15.2 %slice-start.1 = ((bf16[2,64,1792]{2,1,0:T(8,128)(2,1)}), bf16[2,64,256]{2,1,0:T(8,128)(2,1)S(1)}, s32[]{:S(2)}) async-start(bf16[2,64,1792]{2,1,0:T(8,128)(2,1)} %copy-done.7), calls=%async_computation.9 | async-start | bytes 131072 | tf_op jit(solution)/shard_map/slice | solution.py:70
  158.2 15.3 %copy-start.6 = (bf16[2,255,256]{2,1,0:T(8,128)(2,1)S(1)}, bf16[2,255,256]{2,1,0:T(8,128)(2,1)}, u32[]{:S(2)}) copy-start(bf16[2,255,256]{2,1,0:T(8,128)(2,1)} %get-tuple-element.51) | copy-start | bytes 783364
  158.2 15.4 %copy-start.10 = (bf16[256,1,256]{2,0,1:T(8,128)(2,1)S(1)}, bf16[256,1,256]{2,0,1:T(8,128)(2,1)}, u32[]{:S(2)}) copy-start(bf16[256,1,256]{2,0,1:T(8,128)(2,1)} %get-tuple-element.54) | copy-start | bytes 393220
  158.2 61.8 %reduce-scatter.11.cloned.1.call-start = ((), (), s32[]{:S(2)}) async-start(), calls=%async_computation.7 | async-start | bytes 655360 | tf_op jit(solution)/shard_map/reduce_scatter | solution.py:83
  159.1 11.7 %collective-permute-start.9 = (bf16[2,256,256]{2,1,0:T(8,128)(2,1)S(1)}, bf16[2,256,256]{2,1,0:T(8,128)(2,1)S(1)}, u32[]{:S(2)}, u32[]{:S(2)}) collective-permute-start(bf16[2,256,256]{2,1,0:T(8,128)(2,1)S(1)} %copy-done.9), channel_id=1, source_target_pairs={{0,4},{4,8},{8,12},{1,5},{5,9},{9,13},{2,6},{6,10},{10,14},{3,7},{... | collective-permute-start | bytes 786440 | tf_op jit(solution)/shard_map/ppermute | solution.py:12
  193.5 26.5 %copy-start.3 = (bf16[2,64,2048]{2,1,0:T(8,128)(2,1)S(1)}, bf16[2,64,2048]{2,1,0:T(8,128)(2,1)}, u32[]{:S(2)}) copy-start(bf16[2,64,2048]{2,1,0:T(8,128)(2,1)} %copy-done.2) | copy-start | bytes 1572868
  193.5 26.5 %copy-start.12 = (bf16[2,64,2048]{2,1,0:T(8,128)(2,1)S(1)}, bf16[2,64,2048]{2,1,0:T(8,128)(2,1)}, u32[]{:S(2)}) copy-start(bf16[2,64,2048]{2,1,0:T(8,128)(2,1)} %param.12) | copy-start | bytes 1572868
  193.5 26.5 %copy-start.13 = (f32[2,1,64,768]{3,2,0,1:T(8,128)S(1)}, f32[2,1,64,768]{3,2,0,1:T(8,128)}, u32[]{:S(2)}) copy-start(f32[2,1,64,768]{3,2,0,1:T(8,128)} %reduce-scatter.7.cloned.1.call-done) | copy-start | bytes 1179652
  193.5 26.4 %copy-start.14 = (f32[2048]{0:T(1024)S(1)}, f32[2048]{0:T(1024)}, u32[]{:S(2)}) copy-start(f32[2048]{0:T(1024)} %param.13) | copy-start | bytes 24580
  (7 other events, 16.9 us)
Sparse Core Ops, SparseCore 0:
  57.0 23.4 reduce-scatter.4
  112.3 35.0 reduce-scatter.6
  158.3 35.0 reduce-scatter.8
  196.2 23.7 reduce-scatter.10
where the time goes:
time: 230 us; the launch traced here: 229 us
  matrix products  119 us (52%)
  waiting for transfers between devices  38.1 us (17%)
  starting transfers between devices  26.6 us (12%)
  local copies, waits for them, and re-layouts  23.2 us (10%)
  between operations  14.2 us (6%)
  other arithmetic  7.97 us (3%)
    conv_general_dilated x4, matrix products, correlate(): lax.conv_general_dilated(signal, kernel[:, None, :], (1,), 'VALID', dimen...  116 us
    reduce_scatter x4, waiting for transfers between devices, per_device(): reduced = lax.psum_scatter(blocks, 'seq', scatter_dimension=1, tiled=True)  29.3 us
    ppermute x4, starting transfers between devices, from_behind(): return lax.ppermute(block, axis, route)  18.3 us
    slice x14, local copies, waits for them, and re-layouts, per_device(): part[:, :, rest_cols]  9.71 us
    ppermute x4, waiting for transfers between devices, from_behind(): return lax.ppermute(block, axis, route)  8.77 us
  transfers between devices with their start and end apart: 14, of which 3 were waited for; matrix products, arithmetic and copies ran while one was open for 62% of the time, Pallas kernels for 0%

commit v1 on v0

--- a/solution.py
+++ b/solution.py
@@ -3,7 +3,7 @@
 from jax import lax
 from jax.sharding import PartitionSpec as P
 
-CHUNK_PARTS = (1, 3, 3, 1)
+CHUNK_PARTS = (3, 3, 2)
 
 
 def from_behind(block, axis, distance):

time: 230 us -> 218 us (0.948)
  local copies, waits for them, and re-layouts: 23.2 us -> 16.9 us
  starting transfers between devices: 26.6 us -> 20.7 us
    slice x14, local copies, waits for them, and re-layouts: 9.71 us -> 0.89 us  [per_device(): part[:, :, rest_cols]]
    ppermute x4 -> x3, starting transfers between devices: 18.3 us -> 12.5 us  [from_behind(): return lax.ppermute(block, axis, route)]
    unnamed x30 -> x40, local copies, waits for them, and re-layouts: 1.95 us -> 5.64 us
    reduce_scatter x4 -> x3, waiting for transfers between devices: 29.3 us -> 32.5 us  [per_device(): reduced = lax.psum_scatter(blocks, 'seq', scatter_dimension=1, tiled=True)]
    ppermute x4 -> x3, waiting for transfers between devices: 8.77 us -> 6.34 us  [from_behind(): return lax.ppermute(block, axis, route)]
    conv_general_dilated x4 -> x3, matrix products: 116 us -> 116 us  [correlate(): lax.conv_general_dilated(signal, kernel[:, None, :], (1,), 'VALID', dimen...]
  transfers between devices with their start and end apart: 14 -> 12, of which waited for: 3 -> 3; matrix products, arithmetic and copies ran while one was open for 62% -> 61% of each run, Pallas kernels for 0% -> 0%
where the time goes in v1:
time: 218 us; the launch traced here: 217 us
  matrix products  119 us (55%)
  waiting for transfers between devices  38.9 us (18%)
  starting transfers between devices  20.7 us (9%)
  local copies, waits for them, and re-layouts  16.9 us (8%)
  between operations  14.2 us (7%)
  other arithmetic  7.17 us (3%)
    conv_general_dilated x3, matrix products, correlate(): lax.conv_general_dilated(signal, kernel[:, None, :], (1,), 'VALID', dimen...  116 us
    reduce_scatter x3, waiting for transfers between devices, per_device(): reduced = lax.psum_scatter(blocks, 'seq', scatter_dimension=1, tiled=True)  32.5 us
    ppermute x3, starting transfers between devices, from_behind(): return lax.ppermute(block, axis, route)  12.5 us
    ppermute x3, waiting for transfers between devices, from_behind(): return lax.ppermute(block, axis, route)  6.34 us
    unnamed x40, local copies, waits for them, and re-layouts  5.64 us
  transfers between devices with their start and end apart: 12, of which 3 were waited for; matrix products, arithmetic and copies ran while one was open for 61% of the time, Pallas kernels for 0%

profile of v1, /device:TPU:0, one launch (start us, length us, event | category | flops | bytes accessed | tf_op | source)
XLA Modules:
  0.0 217.1 jit_solution(824000130704435056)
XLA Ops:
  7.2 1.5 multiply_convert_fusion
  9.8 1.3 collective-permute-start.2
  11.1 1.3 collective-permute-start.1
  12.4 1.3 collective-permute-start
  13.8 1.3 collective-permute-start.5
  15.1 1.3 fusion.27
  16.4 5.9 %collective-permute-start.3 = (bf16[2,256,768]{2,1,0:T(8,128)(2,1)}, bf16[2,256,768]{2,1,0:T(8,128)(2,1)}, u32[]{:S(2)}, u32[]{:S(2)}) collective-permute-start(bf16[2,256,768]{2,1,0:T(8,128)(2,1)} %get-tuple-element.34), channel_id=1, source_target_pairs={{0,4},{4,8},{8,12},{1,5},{5,9},{9,13},{2,6},{6,10},{10,14},{3,7},{... | collective-permute-start | bytes 2359304 | tf_op jit(solution)/shard_map/ppermute | solution.py:12
  26.3 1.5 fusion.26
  28.6 1.3 collective-permute-start.6
  29.9 1.3 collective-permute-start.7
  31.2 2.1 collective-permute-start.8
  33.3 6.3 %collective-permute-done.3 = bf16[2,256,768]{2,1,0:T(8,128)(2,1)} collective-permute-done((bf16[2,256,768]{2,1,0:T(8,128)(2,1)}, bf16[2,256,768]{2,1,0:T(8,128)(2,1)}, u32[]{:S(2)}, u32[]{:S(2)}) %collective-permute-start.3) | collective-permute-done | bytes 786464 | tf_op jit(solution)/shard_map/ppermute | solution.py:12
  39.6 4.4 %collective-permute-start.4 = (bf16[2,256,768]{2,1,0:T(8,128)(2,1)S(1)}, bf16[2,256,768]{2,1,0:T(8,128)(2,1)S(1)}, u32[]{:S(2)}, u32[]{:S(2)}) collective-permute-start(bf16[2,256,768]{2,1,0:T(8,128)(2,1)S(1)} %copy-done.11), channel_id=1, source_target_pairs={{0,4},{4,8},{8,12},{1,5},{5,9},{9,13},{2,6},{6,10},{10,14},{3,7},{... | collective-permute-start | bytes 2359304 | tf_op jit(solution)/shard_map/ppermute | solution.py:12
  44.1 2.2 %broadcast_select_fusion.2 = (bf16[2,256,768]{2,1,0:T(8,128)(2,1)S(1)}, bf16[2,256,768]{2,1,0:T(8,128)(2,1)}) fusion(pred[2,256]{1,0:T(4,128)(4,1)S(1)} %get-tuple-element.38, bf16[2,256,768]{2,1,0:T(8,128)(2,1)} %collective-permute-done.3, bf16[2,64,768]{2,1,0:T(8,128)(2,1)S(1)} %slice.82, bf16[2,64,768]{2,1,0:T(8,128)(2,1)S(1)} %collective-permute-done.2, ...), kind=kLoop, calls=%fused_computation.28 | loop fusion | flops 3932160 | bytes 3146241 | tf_op jit(solution)/shard_map/jit(_where)/select_n | solution.py:76
  46.4 43.6 %fusion.6 = f32[2,256,768]{2,0,1:T(2,128)S(1)} fusion(bf16[2,511,768]{2,1,0:T(8,128)(2,1)S(1)} %pad_maximum_fusion.1, bf16[256,1,768]{2,0,1:T(8,128)(2,1)S(1)} %get-tuple-element.37), kind=kOutput, calls=%fused_computation.12 | convolution fusion | flops 201326592 | bytes 3535872 | tf_op jit(solution)/shard_map/conv_general_dilated | solution.py:17
  91.3 1.3 rev.9
  94.0 1.1 broadcast_select_fusion.1
  96.2 43.5 %fusion.4 = f32[2,256,768]{2,0,1:T(2,128)S(1)} fusion(bf16[2,511,768]{2,1,0:T(8,128)(2,1)S(1)} %pad_maximum_fusion.2, bf16[256,1,768]{2,0,1:T(8,128)(2,1)S(1)} %copy-done.16), kind=kOutput, calls=%fused_computation.10 | convolution fusion | flops 201326592 | bytes 3535872 | tf_op jit(solution)/shard_map/conv_general_dilated | solution.py:17
  139.9 1.3 rev.10
  143.2 29.1 %fusion.13 = f32[2,256,512]{2,0,1:T(2,128)S(1)} fusion(bf16[2,511,512]{2,1,0:T(8,128)(2,1)S(1)} %pad_maximum_fusion.3, bf16[256,1,512]{2,0,1:T(8,128)(2,1)S(1)} %copy-done.17), kind=kOutput, calls=%fused_computation.21 | convolution fusion | flops 134217728 | bytes 2357248 | tf_op jit(solution)/shard_map/conv_general_dilated | solution.py:17
  173.7 5.7 %reduce-scatter.6.cloned.1.call-done = f32[2,1,64,768]{3,2,0,1:T(8,128)} async-done(((f32[2,4,64,768]{3,2,0,1:T(8,128)}), f32[2,1,64,768]{3,2,0,1:T(8,128)}) %reduce-scatter.6.cloned.1.call-update) | async-done | bytes 393232 | tf_op jit(solution)/shard_map/reduce_scatter | solution.py:83
  179.5 1.6 pad_maximum_fusion
  181.1 26.7 %reduce-scatter.8.cloned.1.call-done = f32[2,1,64,512]{3,2,0,1:T(8,128)} async-done(((f32[2,4,64,512]{3,2,0,1:T(8,128)}), f32[2,1,64,512]{3,2,0,1:T(8,128)}) %reduce-scatter.8.cloned.1.call-update) | async-done | bytes 262160 | tf_op jit(solution)/shard_map/reduce_scatter | solution.py:83
  207.8 2.7 %fusion.2 = bf16[2,64,2048]{2,1,0:T(8,128)(2,1)} fusion(f32[2,64,512]{2,1,0:T(8,128)} %bitcast.32, f32[2,64,768]{2,1,0:T(8,128)} %bitcast.31, f32[2,64,768]{2,1,0:T(8,128)S(1)} %bitcast.30, bf16[2,64,2048]{2,1,0:T(8,128)(2,1)S(1)} %copy-done.3, bf16[2,64,2048]{2,1,0:T(8,128)(2,1)S(1)} %copy-done.14, f32[2048]{0:T(1024)S(1)} %copy-done.18), kind=kOutput, calls=%fused_computation.3 | convolution fusion | flops 203431936 | bytes 2629632 | tf_op jit(solution)/shard_map/ik,rkc->ric/dot_general | solution.py:85
  (87 shorter events, 13.1 us)
Async XLA Ops:
  7.2 7.9 %copy-start = (bf16[2,256,2048]{2,1,0:T(8,128)(2,1)S(1)}, bf16[2,256,2048]{2,1,0:T(8,128)(2,1)}, u32[]{:S(2)}) copy-start(bf16[2,256,2048]{2,1,0:T(8,128)(2,1)} %param.7) | copy-start | bytes 6291460
  7.2 135.2 %reduce-scatter.4.cloned.1.call-start = ((), (), s32[]{:S(2)}) async-start(), calls=%async_computation.3 | async-start | bytes 1966080 | tf_op jit(solution)/shard_map/reduce_scatter | solution.py:83
  9.8 18.8 %collective-permute-start.2 = (bf16[2,64,768]{2,1,0:T(8,128)(2,1)S(1)}, bf16[2,64,768]{2,1,0:T(8,128)(2,1)S(1)}, u32[]{:S(2)}, u32[]{:S(2)}) collective-permute-start(bf16[2,64,768]{2,1,0:T(8,128)(2,1)S(1)} %slice.82), channel_id=1, source_target_pairs={{4,0},{5,1},{6,2},{7,3},{20,16},{21,17},{22,18},{23,19}} | collective-permute-start | bytes 589832 | tf_op jit(solution)/shard_map/ppermute | solution.py:50
  11.1 18.8 %collective-permute-start.1 = (bf16[2,64,768]{2,1,0:T(8,128)(2,1)S(1)}, bf16[2,64,768]{2,1,0:T(8,128)(2,1)}, u32[]{:S(2)}, u32[]{:S(2)}) collective-permute-start(bf16[2,64,768]{2,1,0:T(8,128)(2,1)S(1)} %slice.82), channel_id=1, source_target_pairs={{8,0},{9,1},{10,2},{11,3},{24,16},{25,17},{26,18},{27,19}} | collective-permute-start | bytes 589832 | tf_op jit(solution)/shard_map/ppermute | solution.py:50
  12.4 18.8 %collective-permute-start = (bf16[2,64,768]{2,1,0:T(8,128)(2,1)S(1)}, bf16[2,64,768]{2,1,0:T(8,128)(2,1)}, u32[]{:S(2)}, u32[]{:S(2)}) collective-permute-start(bf16[2,64,768]{2,1,0:T(8,128)(2,1)S(1)} %slice.82), channel_id=1, source_target_pairs={{12,0},{13,1},{14,2},{15,3},{28,16},{29,17},{30,18},{31,19}} | collective-permute-start | bytes 589832 | tf_op jit(solution)/shard_map/ppermute | solution.py:50
  13.8 8.5 %copy-start.19 = (s32[2]{0:T(128)S(1)}, s32[2]{0:T(128)}, u32[]{:S(2)}) copy-start(s32[2]{0:T(128)} %param.9) | copy-start | bytes 28
  13.8 76.2 %collective-permute-start.5 = (bf16[2,64,1280]{2,1,0:T(8,128)(2,1)S(1)}, bf16[2,64,1280]{2,1,0:T(8,128)(2,1)S(1)}, u32[]{:S(2)}, u32[]{:S(2)}) collective-permute-start(bf16[2,64,1280]{2,1,0:T(8,128)(2,1)S(1)} %slice.84), channel_id=1, source_target_pairs={{4,0},{5,1},{6,2},{7,3},{20,16},{21,17},{22,18},{23,19}} | collective-permute-start | bytes 983048 | tf_op jit(solution)/shard_map/ppermute | solution.py:53
  16.4 23.3 %collective-permute-start.3 = (bf16[2,256,768]{2,1,0:T(8,128)(2,1)}, bf16[2,256,768]{2,1,0:T(8,128)(2,1)}, u32[]{:S(2)}, u32[]{:S(2)}) collective-permute-start(bf16[2,256,768]{2,1,0:T(8,128)(2,1)} %get-tuple-element.34), channel_id=1, source_target_pairs={{0,4},{4,8},{8,12},{1,5},{5,9},{9,13},{2,6},{6,10},{10,14},{3,7},{... | collective-permute-start | bytes 2359304 | tf_op jit(solution)/shard_map/ppermute | solution.py:12
  22.6 1.5 copy-start.1
  24.1 1.4 copy-start.7
  26.3 13.3 %copy-start.11 = (bf16[2,256,768]{2,1,0:T(8,128)(2,1)S(1)}, bf16[2,256,768]{2,1,0:T(8,128)(2,1)}, u32[]{:S(2)}) copy-start(bf16[2,256,768]{2,1,0:T(8,128)(2,1)} %get-tuple-element.35) | copy-start | bytes 2359300
  28.6 61.4 %collective-permute-start.6 = (bf16[2,64,1280]{2,1,0:T(8,128)(2,1)S(1)}, bf16[2,64,1280]{2,1,0:T(8,128)(2,1)S(1)}, u32[]{:S(2)}, u32[]{:S(2)}) collective-permute-start(bf16[2,64,1280]{2,1,0:T(8,128)(2,1)S(1)} %slice.84), channel_id=1, source_target_pairs={{8,0},{9,1},{10,2},{11,3},{24,16},{25,17},{26,18},{27,19}} | collective-permute-start | bytes 983048 | tf_op jit(solution)/shard_map/ppermute | solution.py:53
  29.9 60.1 %collective-permute-start.7 = (bf16[2,64,1280]{2,1,0:T(8,128)(2,1)S(1)}, bf16[2,64,1280]{2,1,0:T(8,128)(2,1)S(1)}, u32[]{:S(2)}, u32[]{:S(2)}) collective-permute-start(bf16[2,64,1280]{2,1,0:T(8,128)(2,1)S(1)} %slice.84), channel_id=1, source_target_pairs={{12,0},{13,1},{14,2},{15,3},{28,16},{29,17},{30,18},{31,19}} | collective-permute-start | bytes 983048 | tf_op jit(solution)/shard_map/ppermute | solution.py:53
  31.2 108.5 %collective-permute-start.8 = (bf16[2,256,512]{2,1,0:T(8,128)(2,1)}, bf16[2,256,512]{2,1,0:T(8,128)(2,1)}, u32[]{:S(2)}, u32[]{:S(2)}) collective-permute-start(bf16[2,256,512]{2,1,0:T(8,128)(2,1)} %slice.75), channel_id=1, source_target_pairs={{0,4},{4,8},{8,12},{1,5},{5,9},{9,13},{2,6},{6,10},{10,14},{3,7},{... | collective-permute-start | bytes 1572872 | tf_op jit(solution)/shard_map/ppermute | solution.py:12
  39.6 50.4 %collective-permute-start.4 = (bf16[2,256,768]{2,1,0:T(8,128)(2,1)S(1)}, bf16[2,256,768]{2,1,0:T(8,128)(2,1)S(1)}, u32[]{:S(2)}, u32[]{:S(2)}) collective-permute-start(bf16[2,256,768]{2,1,0:T(8,128)(2,1)S(1)} %copy-done.11), channel_id=1, source_target_pairs={{0,4},{4,8},{8,12},{1,5},{5,9},{9,13},{2,6},{6,10},{10,14},{3,7},{... | collective-permute-start | bytes 2359304 | tf_op jit(solution)/shard_map/ppermute | solution.py:12
  92.6 1.4 copy-start.13
  92.7 86.7 %reduce-scatter.6.cloned.1.call-start = ((), (), s32[]{:S(2)}) async-start(), calls=%async_computation.4 | async-start | bytes 1966080 | tf_op jit(solution)/shard_map/reduce_scatter | solution.py:83
  142.4 65.4 %reduce-scatter.8.cloned.1.call-start = ((), (), s32[]{:S(2)}) async-start(), calls=%async_computation.5 | async-start | bytes 1310720 | tf_op jit(solution)/shard_map/reduce_scatter | solution.py:83
  172.5 6.8 %copy-start.4 = (bf16[2,256,768]{2,1,0:T(8,128)(2,1)S(1)}, bf16[2,256,768]{2,1,0:T(8,128)(2,1)}, u32[]{:S(2)}) copy-start(bf16[2,256,768]{2,1,0:T(8,128)(2,1)} %get-tuple-element.31) | copy-start | bytes 2359300
  172.6 6.8 %copy-start.5 = (bf16[2,256,768]{2,1,0:T(8,128)(2,1)S(1)}, bf16[2,256,768]{2,1,0:T(8,128)(2,1)}, u32[]{:S(2)}) copy-start(bf16[2,256,768]{2,1,0:T(8,128)(2,1)} %get-tuple-element.29) | copy-start | bytes 2359300
  179.4 28.4 %copy-start.3 = (bf16[2,64,2048]{2,1,0:T(8,128)(2,1)S(1)}, bf16[2,64,2048]{2,1,0:T(8,128)(2,1)}, u32[]{:S(2)}) copy-start(bf16[2,64,2048]{2,1,0:T(8,128)(2,1)} %copy-done.2) | copy-start | bytes 1572868
  179.4 28.4 %copy-start.14 = (bf16[2,64,2048]{2,1,0:T(8,128)(2,1)S(1)}, bf16[2,64,2048]{2,1,0:T(8,128)(2,1)}, u32[]{:S(2)}) copy-start(bf16[2,64,2048]{2,1,0:T(8,128)(2,1)} %param.12) | copy-start | bytes 1572868
  179.4 28.4 %copy-start.15 = (f32[2,1,64,768]{3,2,0,1:T(8,128)S(1)}, f32[2,1,64,768]{3,2,0,1:T(8,128)}, u32[]{:S(2)}) copy-start(f32[2,1,64,768]{3,2,0,1:T(8,128)} %reduce-scatter.4.cloned.1.call-done) | copy-start | bytes 1179652
  179.4 28.4 %copy-start.18 = (f32[2048]{0:T(1024)S(1)}, f32[2048]{0:T(1024)}, u32[]{:S(2)}) copy-start(f32[2048]{0:T(1024)} %param.13) | copy-start | bytes 24580
  (14 other events, 14.9 us)
Sparse Core Ops, SparseCore 0:
  92.8 36.4 reduce-scatter.3
  142.5 36.7 reduce-scatter.5
  181.7 26.0 reduce-scatter.7

commit v2 on v1

--- a/solution.py
+++ b/solution.py
@@ -3,7 +3,7 @@
 from jax import lax
 from jax.sharding import PartitionSpec as P
 
-CHUNK_PARTS = (3, 3, 2)
+CHUNK_PARTS = (1, 2, 3, 2)
 
 
 def from_behind(block, axis, distance):

time: 218 us -> 237 us (1.087)
  waiting for transfers between devices: 38.9 us -> 46.6 us
  starting transfers between devices: 20.7 us -> 26.4 us
  matrix products: 119 us -> 122 us
    ppermute x3 -> x4, starting transfers between devices: 12.5 us -> 17.9 us  [from_behind(): return lax.ppermute(block, axis, route)]
    reduce_scatter x3 -> x4, waiting for transfers between devices: 32.5 us -> 37.6 us  [per_device(): reduced = lax.psum_scatter(blocks, 'seq', scatter_dimension=1, tiled=True)]
    unnamed x40 -> x36, local copies, waits for them, and re-layouts: 5.64 us -> 1.86 us
    slice x14, local copies, waits for them, and re-layouts: 0.89 us -> 3.79 us  [per_device(): part[:, :, rest_cols]]
    conv_general_dilated x3 -> x4, matrix products: 116 us -> 119 us  [correlate(): lax.conv_general_dilated(signal, kernel[:, None, :], (1,), 'VALID', dimen...]
    ppermute x3 -> x4, waiting for transfers between devices: 6.34 us -> 8.98 us  [from_behind(): return lax.ppermute(block, axis, route)]
  transfers between devices with their start and end apart: 12 -> 14, of which waited for: 3 -> 3; matrix products, arithmetic and copies ran while one was open for 61% -> 60% of each run, Pallas kernels for 0% -> 0%
where the time goes in v2:
time: 237 us; the launch traced here: 236 us
  matrix products  122 us (51%)
  waiting for transfers between devices  46.6 us (20%)
  starting transfers between devices  26.4 us (11%)
  local copies, waits for them, and re-layouts  18.3 us (8%)
  between operations  14.3 us (6%)
  other arithmetic  8.86 us (4%)
    conv_general_dilated x4, matrix products, correlate(): lax.conv_general_dilated(signal, kernel[:, None, :], (1,), 'VALID', dimen...  119 us
    reduce_scatter x4, waiting for transfers between devices, per_device(): reduced = lax.psum_scatter(blocks, 'seq', scatter_dimension=1, tiled=True)  37.6 us
    ppermute x4, starting transfers between devices, from_behind(): return lax.ppermute(block, axis, route)  17.9 us
    ppermute x4, waiting for transfers between devices, from_behind(): return lax.ppermute(block, axis, route)  8.98 us
  transfers between devices with their start and end apart: 14, of which 3 were waited for; matrix products, arithmetic and copies ran while one was open for 60% of the time, Pallas kernels for 0%

profile of v2, /device:TPU:0, one launch (start us, length us, event | category | flops | bytes accessed | tf_op | source)
XLA Modules:
  0.0 236.5 jit_solution(9796499162705890680)
XLA Ops:
  7.2 1.5 multiply_convert_fusion
  10.4 1.4 collective-permute-start.2
  11.8 1.3 collective-permute-start.1
  13.1 1.3 collective-permute-start
  15.2 6.2 %collective-permute-start.3 = (bf16[2,256,256]{2,1,0:T(8,128)(2,1)}, bf16[2,256,256]{2,1,0:T(8,128)(2,1)}, u32[]{:S(2)}, u32[]{:S(2)}) collective-permute-start(bf16[2,256,256]{2,1,0:T(8,128)(2,1)} %slice.85), channel_id=1, source_target_pairs={{0,4},{4,8},{8,12},{1,5},{5,9},{9,13},{2,6},{6,10},{10,14},{3,7},{... | collective-permute-start | bytes 786440 | tf_op jit(solution)/shard_map/ppermute | solution.py:12
  21.4 1.3 collective-permute-start.7
  23.8 1.8 slice_bitcast_fusion
  29.9 1.3 collective-permute-start.6
  31.2 1.3 collective-permute-start.5
  32.5 6.2 %collective-permute-start.8 = (bf16[2,256,768]{2,1,0:T(8,128)(2,1)}, bf16[2,256,768]{2,1,0:T(8,128)(2,1)}, u32[]{:S(2)}, u32[]{:S(2)}) collective-permute-start(bf16[2,256,768]{2,1,0:T(8,128)(2,1)} %slice.96), channel_id=1, source_target_pairs={{0,4},{4,8},{8,12},{1,5},{5,9},{9,13},{2,6},{6,10},{10,14},{3,7},{... | collective-permute-start | bytes 2359304 | tf_op jit(solution)/shard_map/ppermute | solution.py:12
  38.7 2.7 %collective-permute-start.4 = (bf16[2,256,512]{2,1,0:T(8,128)(2,1)}, bf16[2,256,512]{2,1,0:T(8,128)(2,1)}, u32[]{:S(2)}, u32[]{:S(2)}) collective-permute-start(bf16[2,256,512]{2,1,0:T(8,128)(2,1)} %get-tuple-element.48), channel_id=1, source_target_pairs={{0,4},{4,8},{8,12},{1,5},{5,9},{9,13},{2,6},{6,10},{10,14},{3,7},{... | collective-permute-start | bytes 1572872 | tf_op jit(solution)/shard_map/ppermute | solution.py:12
  41.4 1.7 broadcast_select_fusion.4
  43.1 14.5 %fusion.20 = f32[2,256,256]{2,0,1:T(2,128)S(1)} fusion(bf16[2,511,256]{2,1,0:T(8,128)(2,1)S(1)} %pad_maximum_fusion.4, bf16[256,1,256]{2,0,1:T(8,128)(2,1)S(1)} %copy-done.13), kind=kOutput, calls=%fused_computation.35 | convolution fusion | flops 67108864 | bytes 1178624 | tf_op jit(solution)/shard_map/conv_general_dilated | solution.py:17
  58.7 2.9 %collective-permute-start.9 = (bf16[2,256,512]{2,1,0:T(8,128)(2,1)}, bf16[2,256,512]{2,1,0:T(8,128)(2,1)}, u32[]{:S(2)}, u32[]{:S(2)}) collective-permute-start(bf16[2,256,512]{2,1,0:T(8,128)(2,1)} %get-tuple-element.49), channel_id=1, source_target_pairs={{0,4},{4,8},{8,12},{1,5},{5,9},{9,13},{2,6},{6,10},{10,14},{3,7},{... | collective-permute-start | bytes 1572872 | tf_op jit(solution)/shard_map/ppermute | solution.py:12
  61.6 9.0 %collective-permute-done.4 = bf16[2,256,512]{2,1,0:T(8,128)(2,1)} collective-permute-done((bf16[2,256,512]{2,1,0:T(8,128)(2,1)}, bf16[2,256,512]{2,1,0:T(8,128)(2,1)}, u32[]{:S(2)}, u32[]{:S(2)}) %collective-permute-start.4) | collective-permute-done | bytes 524320 | tf_op jit(solution)/shard_map/ppermute | solution.py:12
  72.6 29.1 %fusion.15 = f32[2,256,512]{2,0,1:T(2,128)S(1)} fusion(bf16[2,511,512]{2,1,0:T(8,128)(2,1)S(1)} %pad_maximum_fusion.2, bf16[256,1,512]{2,0,1:T(8,128)(2,1)S(1)} %copy-done.12), kind=kOutput, calls=%fused_computation.23 | convolution fusion | flops 134217728 | bytes 2357248 | tf_op jit(solution)/shard_map/conv_general_dilated | solution.py:17
  106.2 1.2 pad_maximum_fusion.1
  107.7 46.2 %fusion.4 = f32[2,256,768]{2,0,1:T(2,128)S(1)} fusion(bf16[2,511,768]{2,1,0:T(8,128)(2,1)} %pad_maximum_fusion.1, bf16[256,1,768]{2,0,1:T(8,128)(2,1)S(1)} %copy-done.10), kind=kOutput, calls=%fused_computation.9 | convolution fusion | flops 201326592 | bytes 3535872 | tf_op jit(solution)/shard_map/conv_general_dilated | solution.py:17
  155.1 1.3 rev.14
  157.5 29.1 %fusion.13 = f32[2,256,512]{2,0,1:T(2,128)S(1)} fusion(bf16[2,511,512]{2,1,0:T(8,128)(2,1)S(1)} %pad_maximum_fusion.3, bf16[256,1,512]{2,0,1:T(8,128)(2,1)S(1)} %copy-done.11), kind=kOutput, calls=%fused_computation.21 | convolution fusion | flops 134217728 | bytes 2357248 | tf_op jit(solution)/shard_map/conv_general_dilated | solution.py:17
  188.0 10.8 %reduce-scatter.9.cloned.1.call-done = f32[2,1,64,768]{3,2,0,1:T(8,128)} async-done(((f32[2,4,64,768]{3,2,0,1:T(8,128)}), f32[2,1,64,768]{3,2,0,1:T(8,128)}) %reduce-scatter.9.cloned.1.call-update) | async-done | bytes 393232 | tf_op jit(solution)/shard_map/reduce_scatter | solution.py:83
  198.9 1.6 pad_maximum_fusion
  200.5 26.7 %reduce-scatter.11.cloned.1.call-done = f32[2,1,64,512]{3,2,0,1:T(8,128)} async-done(((f32[2,4,64,512]{3,2,0,1:T(8,128)}), f32[2,1,64,512]{3,2,0,1:T(8,128)}) %reduce-scatter.11.cloned.1.call-update) | async-done | bytes 262160 | tf_op jit(solution)/shard_map/reduce_scatter | solution.py:83
  227.2 2.7 %fusion.2 = bf16[2,64,2048]{2,1,0:T(8,128)(2,1)} fusion(f32[2,64,512]{2,1,0:T(8,128)} %bitcast.37, f32[2,64,768]{2,1,0:T(8,128)S(1)} %bitcast.35, f32[2,64,512]{2,1,0:T(8,128)} %bitcast.36, f32[2,64,256]{2,1,0:T(8,128)} %bitcast.38, bf16[2,64,2048]{2,1,0:T(8,128)(2,1)S(1)} %copy-done.3, bf16[2,64,2048]{2,1,0:T(8,128)(2,1)S(1)} %copy-done.15, ...), kind=kOutput, calls=%fused_computation.3 | convolution fusion | flops 203694080 | bytes 2629632 | tf_op jit(solution)/shard_map/ik,rkc->ric/dot_general | solution.py:85
  (96 shorter events, 19.1 us)
Async XLA Ops:
  7.2 100.2 %reduce-scatter.5.cloned.1.call-start = ((), (), s32[]{:S(2)}) async-start(), calls=%async_computation.4 | async-start | bytes 655360 | tf_op jit(solution)/shard_map/reduce_scatter | solution.py:83
  10.4 15.2 %copy-start.14 = (s32[2]{0:T(128)S(1)}, s32[2]{0:T(128)}, u32[]{:S(2)}) copy-start(s32[2]{0:T(128)} %param.9) | copy-start | bytes 28
  10.4 19.5 %collective-permute-start.2 = (bf16[2,64,256]{2,1,0:T(8,128)(2,1)}, bf16[2,64,256]{2,1,0:T(8,128)(2,1)}, u32[]{:S(2)}, u32[]{:S(2)}) collective-permute-start(bf16[2,64,256]{2,1,0:T(8,128)(2,1)} %slice.110), channel_id=1, source_target_pairs={{4,0},{5,1},{6,2},{7,3},{20,16},{21,17},{22,18},{23,19}} | collective-permute-start | bytes 196616 | tf_op jit(solution)/shard_map/ppermute | solution.py:50
  11.8 19.4 %collective-permute-start.1 = (bf16[2,64,256]{2,1,0:T(8,128)(2,1)}, bf16[2,64,256]{2,1,0:T(8,128)(2,1)}, u32[]{:S(2)}, u32[]{:S(2)}) collective-permute-start(bf16[2,64,256]{2,1,0:T(8,128)(2,1)} %slice.110), channel_id=1, source_target_pairs={{8,0},{9,1},{10,2},{11,3},{24,16},{25,17},{26,18},{27,19}} | collective-permute-start | bytes 196616 | tf_op jit(solution)/shard_map/ppermute | solution.py:50
  13.1 19.4 %collective-permute-start = (bf16[2,64,256]{2,1,0:T(8,128)(2,1)}, bf16[2,64,256]{2,1,0:T(8,128)(2,1)}, u32[]{:S(2)}, u32[]{:S(2)}) collective-permute-start(bf16[2,64,256]{2,1,0:T(8,128)(2,1)} %slice.110), channel_id=1, source_target_pairs={{12,0},{13,1},{14,2},{15,3},{28,16},{29,17},{30,18},{31,19}} | collective-permute-start | bytes 196616 | tf_op jit(solution)/shard_map/ppermute | solution.py:50
  15.2 23.5 %collective-permute-start.3 = (bf16[2,256,256]{2,1,0:T(8,128)(2,1)}, bf16[2,256,256]{2,1,0:T(8,128)(2,1)}, u32[]{:S(2)}, u32[]{:S(2)}) collective-permute-start(bf16[2,256,256]{2,1,0:T(8,128)(2,1)} %slice.85), channel_id=1, source_target_pairs={{0,4},{4,8},{8,12},{1,5},{5,9},{9,13},{2,6},{6,10},{10,14},{3,7},{... | collective-permute-start | bytes 786440 | tf_op jit(solution)/shard_map/ppermute | solution.py:12
  21.4 37.2 %collective-permute-start.7 = (bf16[2,64,1792]{2,1,0:T(8,128)(2,1)S(1)}, bf16[2,64,1792]{2,1,0:T(8,128)(2,1)S(1)}, u32[]{:S(2)}, u32[]{:S(2)}) collective-permute-start(bf16[2,64,1792]{2,1,0:T(8,128)(2,1)S(1)} %slice.112), channel_id=1, source_target_pairs={{12,0},{13,1},{14,2},{15,3},{28,16},{29,17},{30,18},{31,19}} | collective-permute-start | bytes 1376264 | tf_op jit(solution)/shard_map/ppermute | solution.py:53
  29.8 13.4 %copy-start.13 = (bf16[256,1,256]{2,0,1:T(8,128)(2,1)S(1)}, bf16[256,1,256]{2,0,1:T(8,128)(2,1)}, u32[]{:S(2)}) copy-start(bf16[256,1,256]{2,0,1:T(8,128)(2,1)} %slice_bitcast_fusion.3) | copy-start | bytes 393220
  29.9 31.7 %collective-permute-start.6 = (bf16[2,64,1792]{2,1,0:T(8,128)(2,1)S(1)}, bf16[2,64,1792]{2,1,0:T(8,128)(2,1)S(1)}, u32[]{:S(2)}, u32[]{:S(2)}) collective-permute-start(bf16[2,64,1792]{2,1,0:T(8,128)(2,1)S(1)} %slice.112), channel_id=1, source_target_pairs={{8,0},{9,1},{10,2},{11,3},{24,16},{25,17},{26,18},{27,19}} | collective-permute-start | bytes 1376264 | tf_op jit(solution)/shard_map/ppermute | solution.py:53
  31.2 30.4 %collective-permute-start.5 = (bf16[2,64,1792]{2,1,0:T(8,128)(2,1)S(1)}, bf16[2,64,1792]{2,1,0:T(8,128)(2,1)}, u32[]{:S(2)}, u32[]{:S(2)}) collective-permute-start(bf16[2,64,1792]{2,1,0:T(8,128)(2,1)S(1)} %slice.112), channel_id=1, source_target_pairs={{4,0},{5,1},{6,2},{7,3},{20,16},{21,17},{22,18},{23,19}} | collective-permute-start | bytes 1376264 | tf_op jit(solution)/shard_map/ppermute | solution.py:53
  32.5 70.6 %collective-permute-start.8 = (bf16[2,256,768]{2,1,0:T(8,128)(2,1)}, bf16[2,256,768]{2,1,0:T(8,128)(2,1)}, u32[]{:S(2)}, u32[]{:S(2)}) collective-permute-start(bf16[2,256,768]{2,1,0:T(8,128)(2,1)} %slice.96), channel_id=1, source_target_pairs={{0,4},{4,8},{8,12},{1,5},{5,9},{9,13},{2,6},{6,10},{10,14},{3,7},{... | collective-permute-start | bytes 2359304 | tf_op jit(solution)/shard_map/ppermute | solution.py:12
  38.7 31.8 %collective-permute-start.4 = (bf16[2,256,512]{2,1,0:T(8,128)(2,1)}, bf16[2,256,512]{2,1,0:T(8,128)(2,1)}, u32[]{:S(2)}, u32[]{:S(2)}) collective-permute-start(bf16[2,256,512]{2,1,0:T(8,128)(2,1)} %get-tuple-element.48), channel_id=1, source_target_pairs={{0,4},{4,8},{8,12},{1,5},{5,9},{9,13},{2,6},{6,10},{10,14},{3,7},{... | collective-permute-start | bytes 1572872 | tf_op jit(solution)/shard_map/ppermute | solution.py:12
  58.6 98.1 %reduce-scatter.7.cloned.1.call-start = ((), (), s32[]{:S(2)}) async-start(), calls=%async_computation.5 | async-start | bytes 1310720 | tf_op jit(solution)/shard_map/reduce_scatter | solution.py:83
  58.7 95.3 %copy-start.8 = (bf16[2,64,1792]{2,1,0:T(8,128)(2,1)}, bf16[2,64,1792]{2,1,0:T(8,128)(2,1)S(1)}, u32[]{:S(2)}) copy-start(bf16[2,64,1792]{2,1,0:T(8,128)(2,1)S(1)} %collective-permute-done.7) | copy-start | bytes 1376260
  58.7 95.3 %collective-permute-start.9 = (bf16[2,256,512]{2,1,0:T(8,128)(2,1)}, bf16[2,256,512]{2,1,0:T(8,128)(2,1)}, u32[]{:S(2)}, u32[]{:S(2)}) collective-permute-start(bf16[2,256,512]{2,1,0:T(8,128)(2,1)} %get-tuple-element.49), channel_id=1, source_target_pairs={{0,4},{4,8},{8,12},{1,5},{5,9},{9,13},{2,6},{6,10},{10,14},{3,7},{... | collective-permute-start | bytes 1572872 | tf_op jit(solution)/shard_map/ppermute | solution.py:12
  107.4 91.4 %reduce-scatter.9.cloned.1.call-start = ((), (), s32[]{:S(2)}) async-start(), calls=%async_computation.6 | async-start | bytes 1966080 | tf_op jit(solution)/shard_map/reduce_scatter | solution.py:83
  156.7 70.5 %reduce-scatter.11.cloned.1.call-start = ((), (), s32[]{:S(2)}) async-start(), calls=%async_computation.7 | async-start | bytes 1310720 | tf_op jit(solution)/shard_map/reduce_scatter | solution.py:83
  186.9 12.0 %copy-start.1 = (bf16[2,256,768]{2,1,0:T(8,128)(2,1)S(1)}, bf16[2,256,768]{2,1,0:T(8,128)(2,1)}, u32[]{:S(2)}) copy-start(bf16[2,256,768]{2,1,0:T(8,128)(2,1)} %get-tuple-element.41) | copy-start | bytes 2359300
  186.9 12.0 %copy-start.5 = (bf16[2,256,512]{2,1,0:T(8,128)(2,1)S(1)}, bf16[2,256,512]{2,1,0:T(8,128)(2,1)}, u32[]{:S(2)}) copy-start(bf16[2,256,512]{2,1,0:T(8,128)(2,1)} %get-tuple-element.43) | copy-start | bytes 1572868
  186.9 12.0 %copy-start.6 = (bf16[2,256,256]{2,1,0:T(8,128)(2,1)S(1)}, bf16[2,256,256]{2,1,0:T(8,128)(2,1)}, u32[]{:S(2)}) copy-start(bf16[2,256,256]{2,1,0:T(8,128)(2,1)} %get-tuple-element.45) | copy-start | bytes 786436
  198.9 28.4 %copy-start.3 = (bf16[2,64,2048]{2,1,0:T(8,128)(2,1)S(1)}, bf16[2,64,2048]{2,1,0:T(8,128)(2,1)}, u32[]{:S(2)}) copy-start(bf16[2,64,2048]{2,1,0:T(8,128)(2,1)} %copy-done.2) | copy-start | bytes 1572868
  198.9 28.4 %copy-start.15 = (bf16[2,64,2048]{2,1,0:T(8,128)(2,1)S(1)}, bf16[2,64,2048]{2,1,0:T(8,128)(2,1)}, u32[]{:S(2)}) copy-start(bf16[2,64,2048]{2,1,0:T(8,128)(2,1)} %param.12) | copy-start | bytes 1572868
  198.9 28.3 %copy-start.16 = (f32[2,1,64,768]{3,2,0,1:T(8,128)S(1)}, f32[2,1,64,768]{3,2,0,1:T(8,128)}, u32[]{:S(2)}) copy-start(f32[2,1,64,768]{3,2,0,1:T(8,128)} %reduce-scatter.9.cloned.1.call-done) | copy-start | bytes 1179652
  198.9 28.3 %copy-start.17 = (f32[2048]{0:T(1024)S(1)}, f32[2048]{0:T(1024)}, u32[]{:S(2)}) copy-start(f32[2048]{0:T(1024)} %param.13) | copy-start | bytes 24580
  (10 other events, 28.3 us)
Sparse Core Ops, SparseCore 0:
  58.7 23.7 reduce-scatter.4
  107.6 32.7 reduce-scatter.6
  156.9 41.9 reduce-scatter.8
  201.1 26.1 reduce-scatter.10
